TPU v7x, 256 devices: a whole 4x4x8 slice. The times are simulated.
256 devices in a mesh: lat: 8 (over y, z_lo), lon: 8 (over x, core), dp: 4 (over z_hi).
Axes of the slice: x: 4, y: 4, z: 8 (z_hi: 4, z_lo: 2; z = z_hi * 2 + z_lo), core: 2. Of those that a mesh axis runs over, the one named last changes fastest.
Arguments:
- state_grid: bfloat16 [4, 384, 768, 128], P('dp', ('lat', 'lon')), may hold values from -6 to 6
- cotangent: bfloat16 [4, 384, 768, 128], P('dp', ('lat', 'lon')), may hold values from -6 to 6
- legendre: bfloat16 [384, 384, 384], P(('lat', 'lon')), may hold values from -0.3125 to 0.3125
- wave_ids: int32 [384], replicated, may hold values from 0 to 383, each once
- weights: bfloat16 [384, 2, 4, 1024], P('lat'), may hold values from -0.75 to 0.75
Outputs:
- input_grad: bfloat16 [4, 384, 768, 128], P('dp', ('lat', 'lon'))
- weight_grad: float32 [384, 2, 4, 1024], P('lat')
Inputs may be any that keep to these rules, and one draw needn't show every extreme that they name: wave_ids[j] is the wavenumber of slot j; each of 0 to 383 stands in exactly one slot.
All inputs are finite; a program needn't handle non-finite values.
Results may differ from a plain program's by a relative error of at most 0.034.
Values may be sent and summed in bfloat16 or wider, within the bound.
No kernel may reach another device: no remote copies, remote signals or barrier semaphores. Data moves between devices by JAX's collectives and lax.ppermute only.
A program may use at most 128 MiB of HBM per device.

v0:
```python
import math
import jax
import jax.numpy as jnp
from jax import lax
from jax.sharding import PartitionSpec as P

NLON = 768
GROUPS = 4
GROUP_WIDTH = 32


def build_tables(wave_ids):
    columns = jnp.arange(NLON, dtype=jnp.int32)
    phase_int = wave_ids[:, None] * columns[None, :] % NLON
    angles = phase_int.astype(jnp.float32) * jnp.float32(2.0 * math.pi / NLON)
    factor = jnp.float32(1.0 / math.sqrt(NLON))
    paired = jnp.stack([jnp.cos(angles) * factor, -jnp.sin(angles) * factor], axis=1)
    forward_table = paired.reshape(2 * wave_ids.shape[0], NLON)
    doubling = jnp.where(wave_ids == 0, 1.0, 2.0).astype(jnp.float32)
    inverse_table = forward_table * jnp.repeat(doubling, 2)[:, None]
    return (forward_table.astype(jnp.bfloat16), inverse_table.astype(jnp.bfloat16))


def build_kernel(weights):
    degree_count = weights.shape[0]
    real_part = weights[:, 0].reshape(degree_count, GROUPS, GROUP_WIDTH, GROUP_WIDTH)
    imag_part = weights[:, 1].reshape(degree_count, GROUPS, GROUP_WIDTH, GROUP_WIDTH)
    upper_rows = jnp.stack([real_part, imag_part], axis=3)
    lower_rows = jnp.stack([-imag_part, real_part], axis=3)
    return jnp.stack([upper_rows, lower_rows], axis=2)


def gelu_slope(branch):
    normal_cdf = 0.5 * (1.0 + lax.erf(branch * (1.0 / math.sqrt(2.0))))
    density = jnp.exp(-0.5 * branch * branch) * (1.0 / math.sqrt(2.0 * math.pi))
    return normal_cdf + branch * density


def shards(state_grid, cotangent, legendre, wave_ids, weights):
    lat_count = lax.axis_size("lat")
    lon_count = lax.axis_size("lon")
    samples, rows_dev, lon_cells, channels = state_grid.shape
    slot_count, lat_cells, degree_count = legendre.shape
    slot_reals = 2 * slot_count
    first_slot = (lax.axis_index("lat") * lon_count + lax.axis_index("lon")) * slot_count
    held_waves = lax.dynamic_slice_in_dim(wave_ids, first_slot, slot_count)
    degree_ids = jnp.arange(degree_count, dtype=jnp.int32)
    masked = jnp.where(
        degree_ids[None, None, :] >= held_waves[:, None, None],
        legendre,
        jnp.zeros((), legendre.dtype),
    )
    slot_order = wave_ids.reshape(lat_count, lon_count, slot_count).transpose(1, 0, 2).reshape(-1)
    forward_table, inverse_table = build_tables(slot_order)
    kernel = build_kernel(weights)

    def analyze(source, twiddle):
        spectra = jnp.einsum(
            "srnc,kn->srkc", source, twiddle, preferred_element_type=jnp.float32
        ).astype(jnp.bfloat16)
        gathered = lax.all_to_all(
            lax.all_to_all(spectra, "lon", split_axis=2, concat_axis=1, tiled=True),
            "lat",
            split_axis=2,
            concat_axis=1,
            tiled=True,
        )
        blocks = gathered.reshape(samples, lat_cells, slot_count, 2 * channels)
        spectral = jnp.einsum("samc,mal->slmc", blocks, masked, preferred_element_type=jnp.float32)
        spectral = spectral.astype(jnp.bfloat16).reshape(
            samples, degree_count, slot_reals, channels
        )
        return lax.all_to_all(spectral, "lat", split_axis=1, concat_axis=2, tiled=True)

    def synthesize(spectral, twiddle):
        joined = lax.all_to_all(spectral, "lat", split_axis=2, concat_axis=1, tiled=True)
        blocks = joined.reshape(samples, degree_count, slot_count, 2 * channels)
        spectra = jnp.einsum(
            "slmc,mal->samc", blocks, masked, preferred_element_type=jnp.float32
        ).astype(jnp.bfloat16)
        spectra = spectra.reshape(samples, lat_cells, slot_reals, channels)
        pencil = lax.all_to_all(
            lax.all_to_all(spectra, "lat", split_axis=1, concat_axis=2, tiled=True),
            "lon",
            split_axis=1,
            concat_axis=2,
            tiled=True,
        )
        return jnp.einsum("srkc,kn->srnc", pencil, twiddle, preferred_element_type=jnp.float32)

    def split_groups(spectral):
        return spectral.reshape(samples, spectral.shape[1], -1, 2, GROUPS, GROUP_WIDTH)

    coef_fwd = analyze(state_grid, forward_table)
    coef_six = split_groups(coef_fwd)
    mixed_coef = jnp.einsum(
        "slmpgi,lgpiqo->slmqgo", coef_six, kernel, preferred_element_type=jnp.float32
    ).astype(jnp.bfloat16)
    branch = synthesize(mixed_coef.reshape(coef_fwd.shape), inverse_table)
    pulled = (cotangent.astype(jnp.float32) * gelu_slope(branch)).astype(jnp.bfloat16)
    back_coef = analyze(pulled, inverse_table)
    back_six = split_groups(back_coef)
    outer_sums = jnp.einsum(
        "slmpgi,slmqgo->lgpiqo", coef_six, back_six, preferred_element_type=jnp.float32
    )
    real_grad = outer_sums[:, :, 0, :, 0, :] + outer_sums[:, :, 1, :, 1, :]
    imag_grad = outer_sums[:, :, 0, :, 1, :] - outer_sums[:, :, 1, :, 0, :]
    local_grad = jnp.stack([real_grad, imag_grad], axis=1).reshape(weights.shape)
    weight_grad = lax.psum(local_grad.astype(jnp.bfloat16), ("lon", "dp")).astype(jnp.float32)
    demixed = jnp.einsum(
        "slmqgo,lgpiqo->slmpgi", back_six, kernel, preferred_element_type=jnp.float32
    ).astype(jnp.bfloat16)
    returned = synthesize(demixed.reshape(back_coef.shape), forward_table)
    input_grad = (cotangent.astype(jnp.float32) + returned).astype(jnp.bfloat16)
    return (input_grad, weight_grad)


def solution(mesh):
    return jax.shard_map(
        shards,
        mesh=mesh,
        in_specs=(
            P("dp", ("lat", "lon"), None, None),
            P("dp", ("lat", "lon"), None, None),
            P(("lat", "lon"), None, None),
            P(),
            P("lat", None, None, None),
        ),
        out_specs=(P("dp", ("lat", "lon"), None, None), P("lat", None, None, None)),
        check_vma=False,
    )
```

profile of v0, /device:TPU:8, one launch (start us, length us, event | category | flops | bytes accessed | tf_op | source)
XLA Modules:
  0.0 725.3 jit_solution(13457028617643623277)
XLA Ops:
  8.2 4.9 cosine_multiply_fusion
  13.3 2.2 copy.215
  15.6 3.7 reshape.366
  19.3 2.4 fusion.14
  22.5 25.9 %all_to_all.192 = bf16[1,6,768,128]{3,1,0,2:T(8,128)(2,1)S(1)} all-to-all(bf16[1,6,768,128]{3,1,0,2:T(8,128)(2,1)S(1)} %copy.223), channel_id=1, replica_groups=mesh['lat'=8,'lon'=8,'dp'=4] {'lon'}, dimensions={2} | all-to-all | bytes 2359296 | tf_op jit(solution)/shard_map/all_to_all | solution.py:62
  48.7 1.5 copy.226
  50.1 6.5 all-to-all-start.1
  57.4 13.8 %all-to-all-done.1 = bf16[1,48,96,128]{3,1,0,2:T(8,128)(2,1)S(1)} async-done(((bf16[1,48,96,128]{3,1,0,2:T(8,128)(2,1)}), bf16[1,48,96,128]{3,1,0,2:T(8,128)(2,1)S(1)}, u32[]{:S(2)}, u32[]{:S(2)}) %all-to-all-start.1) | async-done | bytes 1179680 | tf_op jit(solution)/shard_map/all_to_all | solution.py:61
  71.2 3.0 copy.280
  74.2 4.4 reshape.378
  78.7 3.4 convolution_convert_fusion.1
  82.1 2.9 copy.229
  85.0 6.4 all-to-all-start.2
  92.5 1.6 copy.298
  95.3 2.2 copy.299
  97.5 2.7 maximum_bitcast_fusion
  100.2 3.0 pad_maximum_fusion
  103.2 12.7 %copy.232 = bf16[48,4,2,32,2,32]{3,5,2,4,1,0:T(8,128)(2,1)} copy(bf16[48,4,2,32,2,32]{0,5,4,3,1,2:T(8,128)(2,1)} %pad_maximum_fusion) | data formatting | bytes 3145728 | tf_op jit(solution)/shard_map/stack | solution.py:30
  115.8 1.7 copy.230
  117.6 2.7 copy.231
  120.3 8.3 %copy.270 = bf16[48,48,2,4,32,1]{1,4,2,5,3,0:T(8,128)(2,1)} copy(bf16[48,48,2,4,32,1]{0,4,3,2,1,5:T(8,128)(2,1)} %bitcast.179) | data formatting | bytes 2359296 | tf_op jit(solution)/shard_map/reshape.8
  128.5 6.7 fusion
  135.3 8.3 %copy.234 = bf16[1,48,48,2,4,32]{1,5,4,3,2,0:T(8,128)(2,1)} copy(bf16[1,48,48,2,4,32]{2,5,3,4,1,0:T(8,128)(2,1)} %fusion) | data formatting | bytes 2359296 | tf_op jit(solution)/shard_map/convert_element_type | solution.py:98
  143.5 3.2 copy.235
  146.7 19.4 %all_to_all.193 = bf16[1,48,96,128]{3,1,0,2:T(8,128)(2,1)} all-to-all(bf16[1,48,96,128]{3,1,0,2:T(8,128)(2,1)S(1)} %copy.235), channel_id=1, replica_groups=mesh['lat'=8,'lon'=8,'dp'=4] {'lat'}, dimensions={2} | all-to-all | bytes 2359296 | tf_op jit(solution)/shard_map/all_to_all | solution.py:76
  166.2 4.2 copy.283
  170.4 4.4 reshape.379
  174.8 3.5 convolution_convert_fusion.3
  178.3 2.9 copy.238
  181.2 21.5 %all_to_all.194 = bf16[1,384,12,128]{3,2,0,1:T(8,128)(2,1)S(1)} all-to-all(bf16[1,384,12,128]{3,2,0,1:T(8,128)(2,1)} %copy.238), channel_id=1, replica_groups=mesh['lat'=8,'lon'=8,'dp'=4] {'lat'}, dimensions={1} | all-to-all | bytes 2359296 | tf_op jit(solution)/shard_map/all_to_all | solution.py:83
  204.4 4.3 all-to-all-start.5
  211.1 14.9 %all-to-all-done.5 = bf16[1,48,96,128]{3,2,0,1:T(8,128)(2,1)} async-done(((bf16[1,48,96,128]{3,2,0,1:T(8,128)(2,1)}), bf16[1,48,96,128]{3,2,0,1:T(8,128)(2,1)}, u32[]{:S(2)}, u32[]{:S(2)}) %all-to-all-start.5) | async-done | bytes 1179680 | tf_op jit(solution)/shard_map/all_to_all | solution.py:82
  227.4 4.8 fusion.15
  232.3 2.1 copy.244
  234.4 24.2 %all_to_all.195 = bf16[1,6,768,128]{3,1,0,2:T(8,128)(2,1)S(1)} all-to-all(bf16[1,6,768,128]{3,1,0,2:T(8,128)(2,1)S(1)} %copy.244), channel_id=1, replica_groups=mesh['lat'=8,'lon'=8,'dp'=4] {'lon'}, dimensions={2} | all-to-all | bytes 2359296 | tf_op jit(solution)/shard_map/all_to_all | solution.py:62
  259.3 20.1 %all_to_all.196 = bf16[1,48,96,128]{3,1,0,2:T(8,128)(2,1)S(1)} all-to-all(bf16[1,48,96,128]{3,1,0,2:T(8,128)(2,1)S(1)} %copy.247), channel_id=1, replica_groups=mesh['lat'=8,'lon'=8,'dp'=4] {'lat'}, dimensions={2} | all-to-all | bytes 2359296 | tf_op jit(solution)/shard_map/all_to_all | solution.py:61
  279.4 3.0 copy.284
  282.4 4.4 reshape.380
  286.8 2.4 convolution_convert_fusion
  289.2 2.0 copy.250
  291.1 5.1 all-to-all-start.8
  296.3 11.6 %copy.253 = bf16[48,4,2,32,2,32]{5,3,4,2,1,0:T(8,128)(2,1)} copy(bf16[48,4,2,32,2,32]{0,5,4,3,1,2:T(8,128)(2,1)} %pad_maximum_fusion) | data formatting | bytes 3145728 | tf_op jit(solution)/shard_map/stack | solution.py:30
  307.8 6.3 all-to-all-done.8
  314.5 2.7 copy.252
  317.2 8.3 %copy.273 = bf16[48,48,2,4,32,1]{1,4,2,5,3,0:T(8,128)(2,1)} copy(bf16[48,48,2,4,32,1]{0,4,3,2,1,5:T(8,128)(2,1)} %bitcast.182) | data formatting | bytes 2359296 | tf_op jit(solution)/shard_map/reshape.39
  325.5 6.8 fusion.1
  332.3 8.3 %copy.255 = bf16[1,48,48,2,4,32]{1,5,4,3,2,0:T(8,128)(2,1)} copy(bf16[1,48,48,2,4,32]{2,5,3,4,1,0:T(8,128)(2,1)} %fusion.1) | data formatting | bytes 2359296 | tf_op jit(solution)/shard_map/convert_element_type | solution.py:112
  340.6 3.2 copy.256
  343.8 19.7 %all_to_all.197 = bf16[1,48,96,128]{3,1,0,2:T(8,128)(2,1)S(1)} all-to-all(bf16[1,48,96,128]{3,1,0,2:T(8,128)(2,1)S(1)} %copy.256), channel_id=1, replica_groups=mesh['lat'=8,'lon'=8,'dp'=4] {'lat'}, dimensions={2} | all-to-all | bytes 2359296 | tf_op jit(solution)/shard_map/all_to_all | solution.py:76
  363.5 3.0 copy.287
  366.4 4.4 reshape.381
  370.9 2.4 convolution_convert_fusion.2
  373.3 2.0 copy.259
  375.3 5.3 all-to-all-start.10
  380.6 8.3 %copy.276 = bf16[48,48,2,4,32,1]{1,4,5,2,3,0:T(8,128)(2,1)} copy(bf16[48,48,2,4,32,1]{0,4,3,2,1,5:T(8,128)(2,1)} %bitcast.180) | data formatting | bytes 2359296 | tf_op jit(solution)/shard_map/reshape.8
  388.9 12.5 %fusion.41 = f32[48,4,2,32,2,32]{5,3,4,2,1,0:T(8,128)} fusion(bf16[48,48,2,4,32,1]{1,4,5,2,3,0:T(8,128)(2,1)} %copy.276, bf16[48,48,2,4,32,1]{1,4,2,5,3,0:T(8,128)(2,1)} %copy.273), kind=kOutput, calls=%fused_computation.66 | convolution fusion | flops 75497472 | bytes 5505024 | tf_op jit(solution)/shard_map/slmpgi,slmqgo->lgpiqo/dot_general | solution.py:103
  403.1 4.3 all-to-all-start.11
  407.4 7.5 %fusion.3 = (bf16[48,4,1,32,1,32]{5,3,4,2,1,0:T(8,128)(2,1)}, bf16[48,4,1,32,1,32]{5,3,4,2,1,0:T(8,128)(2,1)S(1)}) fusion(f32[48,4,2,32,2,32]{5,3,4,2,1,0:T(8,128)} %fusion.41), kind=kLoop, calls=%fused_computation.9 | loop fusion | flops 786432 | bytes 3932160 | tf_op jit(solution)/shard_map/convert.3
  415.0 2.9 reshape.382
  418.0 1.5 reshape.383
  421.6 290.0 %all-reduce.2.cloned.1.call-done = bf16[48,2,4,1024]{3,0,2,1:T(8,128)(2,1)} async-done(((bf16[48,2,4,1024]{3,0,2,1:T(8,128)(2,1)}), bf16[48,2,4,1024]{3,0,2,1:T(8,128)(2,1)}) %all-reduce.2.cloned.1.call-update) | async-done | bytes 786448 | tf_op jit(solution)/shard_map/psum | solution.py:109
  711.6 2.9 copy.269
  714.5 1.5 copy.263
  716.1 2.1 fusion.5
  (46 shorter events, 16.0 us)
Async XLA Ops:
  7.2 12.2 %copy-start = (bf16[1,6,768,128]{3,2,1,0:T(8,128)(2,1)S(1)}, bf16[1,6,768,128]{3,2,1,0:T(8,128)(2,1)}, u32[]{:S(2)}) copy-start(bf16[1,6,768,128]{3,2,1,0:T(8,128)(2,1)} %param.5) | copy-start | bytes 3538948
  50.1 21.1 %all-to-all-start.1 = ((bf16[1,48,96,128]{3,1,0,2:T(8,128)(2,1)}), bf16[1,48,96,128]{3,1,0,2:T(8,128)(2,1)S(1)}, u32[]{:S(2)}, u32[]{:S(2)}) async-start(bf16[1,48,96,128]{3,1,0,2:T(8,128)(2,1)} %copy.226), calls=%async_computation.1 | async-start | bytes 2359296 | tf_op jit(solution)/shard_map/all_to_all | solution.py:61
  85.0 6.4 copy-start.3
  85.0 30.9 %all-to-all-start.2 = ((bf16[1,384,12,128]{3,2,0,1:T(8,128)(2,1)}), bf16[1,384,12,128]{3,2,0,1:T(8,128)(2,1)}, u32[]{:S(2)}, u32[]{:S(2)}) async-start(bf16[1,384,12,128]{3,2,0,1:T(8,128)(2,1)} %copy.229), calls=%async_computation.2 | async-start | bytes 3145728 | tf_op jit(solution)/shard_map/all_to_all | solution.py:73
  204.4 21.6 %all-to-all-start.5 = ((bf16[1,48,96,128]{3,2,0,1:T(8,128)(2,1)}), bf16[1,48,96,128]{3,2,0,1:T(8,128)(2,1)}, u32[]{:S(2)}, u32[]{:S(2)}) async-start(bf16[1,48,96,128]{3,2,0,1:T(8,128)(2,1)} %copy.241), calls=%async_computation.5 | async-start | bytes 2359296 | tf_op jit(solution)/shard_map/all_to_all | solution.py:82
  291.1 23.0 %all-to-all-start.8 = ((bf16[1,384,12,128]{3,2,0,1:T(8,128)(2,1)}), bf16[1,384,12,128]{3,2,0,1:T(8,128)(2,1)S(1)}, u32[]{:S(2)}, u32[]{:S(2)}) async-start(bf16[1,384,12,128]{3,2,0,1:T(8,128)(2,1)} %copy.250), calls=%async_computation.8 | async-start | bytes 3145728 | tf_op jit(solution)/shard_map/all_to_all | solution.py:73
  375.3 26.1 %all-to-all-start.10 = ((bf16[1,384,12,128]{3,2,0,1:T(8,128)(2,1)}), bf16[1,384,12,128]{3,2,0,1:T(8,128)(2,1)S(1)}, u32[]{:S(2)}, u32[]{:S(2)}) async-start(bf16[1,384,12,128]{3,2,0,1:T(8,128)(2,1)} %copy.259), calls=%async_computation.10 | async-start | bytes 3145728 | tf_op jit(solution)/shard_map/all_to_all | solution.py:83
  403.1 311.3 %all-to-all-start.11 = ((bf16[1,48,96,128]{3,2,0,1:T(8,128)(2,1)}), bf16[1,48,96,128]{3,2,0,1:T(8,128)(2,1)}, u32[]{:S(2)}, u32[]{:S(2)}) async-start(bf16[1,48,96,128]{3,2,0,1:T(8,128)(2,1)} %copy.262), calls=%async_computation.11 | async-start | bytes 2359296 | tf_op jit(solution)/shard_map/all_to_all | solution.py:82
  407.4 304.2 %all-reduce.2.cloned.1.call-start = ((), (), s32[]{:S(2)}) async-start(), calls=%async_computation.12 | async-start | bytes 1572864 | tf_op jit(solution)/shard_map/psum | solution.py:109
  419.5 1.6 copy-start.2
  714.5 1.6 copy-start.4
  716.1 2.1 copy-start.1
Sparse Core Ops, SparseCore 0:
  420.8 290.7 all-reduce.1
where the time goes:
time: 735 us; the launch traced here: 725 us
  waiting for transfers between devices  325 us (44%)
  local copies, waits for them, and re-layouts  155 us (21%)
  blocking collectives  131 us (18%)
  matrix products  47 us (6%)
  starting transfers between devices  31.8 us (4%)
  other arithmetic  20.7 us (3%)
  between operations  14.6 us (2%)
    psum x1, waiting for transfers between devices, shards(): lax.psum(local_grad.astype(jnp.bfloat16), ('lon', 'dp')).astype(jnp.float32)  290 us
    another operation x11, local copies, waits for them, and re-layouts  55.7 us
    all_to_all x2, blocking collectives, analyze(): lax.all_to_all(spectra, 'lon', split_axis=2, concat_axis=1, tiled=True)  50.1 us
    all_to_all x2, blocking collectives, synthesize(): lax.all_to_all(spectral, 'lat', split_axis=2, concat_axis=1, tiled=True)  39.1 us
    another operation x2, local copies, waits for them, and re-layouts, build_kernel(): return jnp.stack([upper_rows, lower_rows], axis=2)  24.2 us
    all_to_all x1, blocking collectives, synthesize(): lax.all_to_all(spectra, 'lat', split_axis=1, concat_axis=2, tiled=True)  21.5 us
    all_to_all x1, blocking collectives, analyze(): lax.all_to_all(lax.all_to_all(spectra, 'lon', split_axis=2, concat_axis=1...  20.1 us
    all_to_all x2, waiting for transfers between devices, synthesize(): lax.all_to_all(lax.all_to_all(spectra, 'lat', split_axis=1, concat_axis=2...  14.9 us
  transfers between devices with their start and end apart: 7, of which 4 were waited for; matrix products, arithmetic and copies ran while one was open for 11% of the time, Pallas kernels for 0%

commit v1 on v0

--- a/solution.py
+++ b/solution.py
@@ -7,6 +7,13 @@
 NLON = 768
 GROUPS = 4
 GROUP_WIDTH = 32
+
+
+def trade_parts(x, axis, split, join):
+    size = lax.axis_size(axis)
+    pieces = jnp.stack(jnp.split(x, size, axis=split), axis=0)
+    pieces = lax.all_to_all(pieces, axis, split_axis=0, concat_axis=0)
+    return jnp.concatenate(pieces, axis=join)
 
 
 def build_tables(wave_ids):
@@ -58,12 +65,8 @@
         spectra = jnp.einsum(
             "srnc,kn->srkc", source, twiddle, preferred_element_type=jnp.float32
         ).astype(jnp.bfloat16)
-        gathered = lax.all_to_all(
-            lax.all_to_all(spectra, "lon", split_axis=2, concat_axis=1, tiled=True),
-            "lat",
-            split_axis=2,
-            concat_axis=1,
-            tiled=True,
+        gathered = trade_parts(
+            lax.all_to_all(spectra, "lon", split_axis=2, concat_axis=1, tiled=True), "lat", 2, 1
         )
         blocks = gathered.reshape(samples, lat_cells, slot_count, 2 * channels)
         spectral = jnp.einsum("samc,mal->slmc", blocks, masked, preferred_element_type=jnp.float32)

time: 735 us -> 736 us (level)
    another operation x11 -> x15, local copies, waits for them, and re-layouts: 55.7 us -> 57.4 us
where the time goes in v1:
time: 736 us; the launch traced here: 726 us
  waiting for transfers between devices  325 us (44%)
  local copies, waits for them, and re-layouts  156 us (21%)
  blocking collectives  131 us (18%)
  matrix products  47 us (6%)
  starting transfers between devices  31.8 us (4%)
  other arithmetic  20.7 us (3%)
  between operations  14.6 us (2%)
    psum x1, waiting for transfers between devices, shards(): lax.psum(local_grad.astype(jnp.bfloat16), ('lon', 'dp')).astype(jnp.float32)  290 us
    another operation x11, local copies, waits for them, and re-layouts  55.7 us
    all_to_all x2, blocking collectives, analyze(): lax.all_to_all(spectra, 'lon', split_axis=2, concat_axis=1, tiled=True)  50.1 us
    all_to_all x2, blocking collectives, synthesize(): lax.all_to_all(spectral, 'lat', split_axis=2, concat_axis=1, tiled=True)  39.1 us
    another operation x2, local copies, waits for them, and re-layouts, build_kernel(): return jnp.stack([upper_rows, lower_rows], axis=2)  24.2 us
    all_to_all x1, blocking collectives, synthesize(): lax.all_to_all(spectra, 'lat', split_axis=1, concat_axis=2, tiled=True)  21.5 us
    all_to_all x1, blocking collectives, trade_parts(): pieces = lax.all_to_all(pieces, axis, split_axis=0, concat_axis=0)  20.1 us
    all_to_all x2, waiting for transfers between devices, synthesize(): lax.all_to_all(lax.all_to_all(spectra, 'lat', split_axis=1, concat_axis=2...  14.9 us
  transfers between devices with their start and end apart: 7, of which 4 were waited for; matrix products, arithmetic and copies ran while one was open for 11% of the time, Pallas kernels for 0%

profile of v1, /device:TPU:8, one launch (start us, length us, event | category | flops | bytes accessed | tf_op | source)
XLA Modules:
  0.0 726.1 jit_solution(6526665762379113719)
XLA Ops:
  8.2 4.9 cosine_multiply_fusion
  13.3 2.2 copy.241
  15.6 3.7 reshape.362
  19.3 2.4 fusion.14
  22.5 25.9 %all_to_all.172 = bf16[1,6,768,128]{3,1,0,2:T(8,128)(2,1)S(1)} all-to-all(bf16[1,6,768,128]{3,1,0,2:T(8,128)(2,1)S(1)} %copy.249), channel_id=1, replica_groups=mesh['lat'=8,'lon'=8,'dp'=4] {'lon'}, dimensions={2} | all-to-all | bytes 2359296 | tf_op jit(solution)/shard_map/all_to_all | solution.py:69
  50.4 6.5 all-to-all-start.1
  57.8 13.8 %all-to-all-done.1 = bf16[8,1,48,12,128]{4,2,3,1,0:T(8,128)(2,1)S(1)} async-done(((bf16[8,1,48,12,128]{4,2,3,1,0:T(8,128)(2,1)}), bf16[8,1,48,12,128]{4,2,3,1,0:T(8,128)(2,1)S(1)}, u32[]{:S(2)}, u32[]{:S(2)}) %all-to-all-start.1) | async-done | bytes 1179680 | tf_op jit(solution)/shard_map/all_to_all | solution.py:15
  71.5 3.0 copy.311
  74.5 4.4 reshape.374
  79.0 3.4 convolution_convert_fusion.1
  82.4 2.9 copy.257
  85.3 6.4 all-to-all-start.2
  92.8 1.6 copy.330
  95.6 2.2 copy.331
  97.8 2.7 maximum_bitcast_fusion
  100.5 3.0 pad_maximum_fusion
  103.5 12.7 %copy.260 = bf16[48,4,2,32,2,32]{3,5,2,4,1,0:T(8,128)(2,1)} copy(bf16[48,4,2,32,2,32]{0,5,4,3,1,2:T(8,128)(2,1)} %pad_maximum_fusion) | data formatting | bytes 3145728 | tf_op jit(solution)/shard_map/stack | solution.py:37
  116.1 1.7 copy.258
  117.9 2.7 copy.259
  120.6 8.3 %copy.300 = bf16[48,48,2,4,32,1]{1,4,2,5,3,0:T(8,128)(2,1)} copy(bf16[48,48,2,4,32,1]{0,4,3,2,1,5:T(8,128)(2,1)} %bitcast.237) | data formatting | bytes 2359296 | tf_op jit(solution)/shard_map/reshape.7
  128.9 6.7 fusion
  135.6 8.3 %copy.262 = bf16[1,48,48,2,4,32]{1,5,4,3,2,0:T(8,128)(2,1)} copy(bf16[1,48,48,2,4,32]{2,5,3,4,1,0:T(8,128)(2,1)} %fusion) | data formatting | bytes 2359296 | tf_op jit(solution)/shard_map/convert_element_type | solution.py:101
  143.8 3.2 copy.263
  147.0 19.4 %all_to_all.173 = bf16[1,48,96,128]{3,1,0,2:T(8,128)(2,1)} all-to-all(bf16[1,48,96,128]{3,1,0,2:T(8,128)(2,1)S(1)} %copy.263), channel_id=1, replica_groups=mesh['lat'=8,'lon'=8,'dp'=4] {'lat'}, dimensions={2} | all-to-all | bytes 2359296 | tf_op jit(solution)/shard_map/all_to_all | solution.py:79
  166.5 4.2 copy.314
  170.7 4.4 reshape.375
  175.1 3.5 convolution_convert_fusion.3
  178.6 2.9 copy.266
  181.5 21.5 %all_to_all.174 = bf16[1,384,12,128]{3,2,0,1:T(8,128)(2,1)S(1)} all-to-all(bf16[1,384,12,128]{3,2,0,1:T(8,128)(2,1)} %copy.266), channel_id=1, replica_groups=mesh['lat'=8,'lon'=8,'dp'=4] {'lat'}, dimensions={1} | all-to-all | bytes 2359296 | tf_op jit(solution)/shard_map/all_to_all | solution.py:86
  204.7 4.3 all-to-all-start.5
  211.4 14.9 %all-to-all-done.5 = bf16[1,48,96,128]{3,2,0,1:T(8,128)(2,1)} async-done(((bf16[1,48,96,128]{3,2,0,1:T(8,128)(2,1)}), bf16[1,48,96,128]{3,2,0,1:T(8,128)(2,1)}, u32[]{:S(2)}, u32[]{:S(2)}) %all-to-all-start.5) | async-done | bytes 1179680 | tf_op jit(solution)/shard_map/all_to_all | solution.py:85
  226.4 1.4 copy.270
  227.7 4.8 fusion.15
  232.6 2.1 copy.272
  234.7 24.2 %all_to_all.175 = bf16[1,6,768,128]{3,1,0,2:T(8,128)(2,1)S(1)} all-to-all(bf16[1,6,768,128]{3,1,0,2:T(8,128)(2,1)S(1)} %copy.272), channel_id=1, replica_groups=mesh['lat'=8,'lon'=8,'dp'=4] {'lon'}, dimensions={2} | all-to-all | bytes 2359296 | tf_op jit(solution)/shard_map/all_to_all | solution.py:69
  259.9 20.1 %all_to_all.176 = bf16[8,1,48,12,128]{4,2,3,1,0:T(8,128)(2,1)S(1)} all-to-all(bf16[8,1,48,12,128]{4,2,3,1,0:T(8,128)(2,1)S(1)} %copy.277), channel_id=1, replica_groups=mesh['lat'=8,'lon'=8,'dp'=4] {'lat'}, dimensions={0} | all-to-all | bytes 2359296 | tf_op jit(solution)/shard_map/all_to_all | solution.py:15
  280.0 3.0 copy.316
  283.0 4.4 reshape.376
  287.4 2.4 convolution_convert_fusion
  289.8 2.0 copy.280
  291.8 5.1 all-to-all-start.8
  296.9 11.6 %copy.283 = bf16[48,4,2,32,2,32]{5,3,4,2,1,0:T(8,128)(2,1)} copy(bf16[48,4,2,32,2,32]{0,5,4,3,1,2:T(8,128)(2,1)} %pad_maximum_fusion) | data formatting | bytes 3145728 | tf_op jit(solution)/shard_map/stack | solution.py:37
  308.5 6.3 all-to-all-done.8
  315.1 2.7 copy.282
  317.8 8.3 %copy.303 = bf16[48,48,2,4,32,1]{1,4,2,5,3,0:T(8,128)(2,1)} copy(bf16[48,48,2,4,32,1]{0,4,3,2,1,5:T(8,128)(2,1)} %bitcast.240) | data formatting | bytes 2359296 | tf_op jit(solution)/shard_map/reshape.35
  326.1 6.8 fusion.1
  332.9 8.3 %copy.285 = bf16[1,48,48,2,4,32]{1,5,4,3,2,0:T(8,128)(2,1)} copy(bf16[1,48,48,2,4,32]{2,5,3,4,1,0:T(8,128)(2,1)} %fusion.1) | data formatting | bytes 2359296 | tf_op jit(solution)/shard_map/convert_element_type | solution.py:115
  341.2 3.2 copy.286
  344.4 19.7 %all_to_all.177 = bf16[1,48,96,128]{3,1,0,2:T(8,128)(2,1)S(1)} all-to-all(bf16[1,48,96,128]{3,1,0,2:T(8,128)(2,1)S(1)} %copy.286), channel_id=1, replica_groups=mesh['lat'=8,'lon'=8,'dp'=4] {'lat'}, dimensions={2} | all-to-all | bytes 2359296 | tf_op jit(solution)/shard_map/all_to_all | solution.py:79
  364.1 3.0 copy.319
  367.0 4.4 reshape.377
  371.5 2.4 convolution_convert_fusion.2
  373.9 2.0 copy.289
  375.9 5.3 all-to-all-start.10
  381.2 8.3 %copy.306 = bf16[48,48,2,4,32,1]{1,4,5,2,3,0:T(8,128)(2,1)} copy(bf16[48,48,2,4,32,1]{0,4,3,2,1,5:T(8,128)(2,1)} %bitcast.238) | data formatting | bytes 2359296 | tf_op jit(solution)/shard_map/reshape.7
  389.5 12.5 %fusion.57 = f32[48,4,2,32,2,32]{5,3,4,2,1,0:T(8,128)} fusion(bf16[48,48,2,4,32,1]{1,4,5,2,3,0:T(8,128)(2,1)} %copy.306, bf16[48,48,2,4,32,1]{1,4,2,5,3,0:T(8,128)(2,1)} %copy.303), kind=kOutput, calls=%fused_computation.98 | convolution fusion | flops 75497472 | bytes 5505024 | tf_op jit(solution)/shard_map/slmpgi,slmqgo->lgpiqo/dot_general | solution.py:106
  403.7 4.3 all-to-all-start.11
  408.0 7.5 %fusion.3 = (bf16[48,4,1,32,1,32]{5,3,4,2,1,0:T(8,128)(2,1)}, bf16[48,4,1,32,1,32]{5,3,4,2,1,0:T(8,128)(2,1)S(1)}) fusion(f32[48,4,2,32,2,32]{5,3,4,2,1,0:T(8,128)} %fusion.57), kind=kLoop, calls=%fused_computation.9 | loop fusion | flops 786432 | bytes 3932160 | tf_op jit(solution)/shard_map/convert.3
  415.6 2.9 reshape.378
  418.6 1.5 reshape.379
  422.1 290.2 %all-reduce.2.cloned.1.call-done = bf16[48,2,4,1024]{3,0,2,1:T(8,128)(2,1)} async-done(((bf16[48,2,4,1024]{3,0,2,1:T(8,128)(2,1)}), bf16[48,2,4,1024]{3,0,2,1:T(8,128)(2,1)}) %all-reduce.2.cloned.1.call-update) | async-done | bytes 786448 | tf_op jit(solution)/shard_map/psum | solution.py:112
  712.4 2.9 copy.299
  715.3 1.5 copy.293
  716.9 2.1 fusion.5
  (62 shorter events, 16.7 us)
Async XLA Ops:
  7.2 12.2 %copy-start = (bf16[1,6,768,128]{3,2,1,0:T(8,128)(2,1)S(1)}, bf16[1,6,768,128]{3,2,1,0:T(8,128)(2,1)}, u32[]{:S(2)}) copy-start(bf16[1,6,768,128]{3,2,1,0:T(8,128)(2,1)} %param.5) | copy-start | bytes 3538948
  50.4 21.1 %all-to-all-start.1 = ((bf16[8,1,48,12,128]{4,2,3,1,0:T(8,128)(2,1)}), bf16[8,1,48,12,128]{4,2,3,1,0:T(8,128)(2,1)S(1)}, u32[]{:S(2)}, u32[]{:S(2)}) async-start(bf16[8,1,48,12,128]{4,2,3,1,0:T(8,128)(2,1)} %copy.254), calls=%async_computation.1 | async-start | bytes 2359296 | tf_op jit(solution)/shard_map/all_to_all | solution.py:15
  85.3 6.4 copy-start.3
  85.3 30.9 %all-to-all-start.2 = ((bf16[1,384,12,128]{3,2,0,1:T(8,128)(2,1)}), bf16[1,384,12,128]{3,2,0,1:T(8,128)(2,1)}, u32[]{:S(2)}, u32[]{:S(2)}) async-start(bf16[1,384,12,128]{3,2,0,1:T(8,128)(2,1)} %copy.257), calls=%async_computation.2 | async-start | bytes 3145728 | tf_op jit(solution)/shard_map/all_to_all | solution.py:76
  204.7 21.6 %all-to-all-start.5 = ((bf16[1,48,96,128]{3,2,0,1:T(8,128)(2,1)}), bf16[1,48,96,128]{3,2,0,1:T(8,128)(2,1)}, u32[]{:S(2)}, u32[]{:S(2)}) async-start(bf16[1,48,96,128]{3,2,0,1:T(8,128)(2,1)} %copy.269), calls=%async_computation.5 | async-start | bytes 2359296 | tf_op jit(solution)/shard_map/all_to_all | solution.py:85
  291.8 23.0 %all-to-all-start.8 = ((bf16[1,384,12,128]{3,2,0,1:T(8,128)(2,1)}), bf16[1,384,12,128]{3,2,0,1:T(8,128)(2,1)S(1)}, u32[]{:S(2)}, u32[]{:S(2)}) async-start(bf16[1,384,12,128]{3,2,0,1:T(8,128)(2,1)} %copy.280), calls=%async_computation.8 | async-start | bytes 3145728 | tf_op jit(solution)/shard_map/all_to_all | solution.py:76
  375.9 26.1 %all-to-all-start.10 = ((bf16[1,384,12,128]{3,2,0,1:T(8,128)(2,1)}), bf16[1,384,12,128]{3,2,0,1:T(8,128)(2,1)S(1)}, u32[]{:S(2)}, u32[]{:S(2)}) async-start(bf16[1,384,12,128]{3,2,0,1:T(8,128)(2,1)} %copy.289), calls=%async_computation.10 | async-start | bytes 3145728 | tf_op jit(solution)/shard_map/all_to_all | solution.py:86
  403.7 311.5 %all-to-all-start.11 = ((bf16[1,48,96,128]{3,2,0,1:T(8,128)(2,1)}), bf16[1,48,96,128]{3,2,0,1:T(8,128)(2,1)}, u32[]{:S(2)}, u32[]{:S(2)}) async-start(bf16[1,48,96,128]{3,2,0,1:T(8,128)(2,1)} %copy.292), calls=%async_computation.11 | async-start | bytes 2359296 | tf_op jit(solution)/shard_map/all_to_all | solution.py:85
  408.0 304.4 %all-reduce.2.cloned.1.call-start = ((), (), s32[]{:S(2)}) async-start(), calls=%async_computation.12 | async-start | bytes 1572864 | tf_op jit(solution)/shard_map/psum | solution.py:112
  420.1 1.6 copy-start.2
  715.3 1.6 copy-start.4
  716.9 2.1 copy-start.1
Sparse Core Ops, SparseCore 0:
  421.3 290.9 all-reduce.1
